TPU v7x, 256 devices: a whole 4x4x8 slice. The times are simulated.
256 devices in a mesh: rows: 16 (over x, y), sub: 16 (over z, core).
Axes of the slice: x: 4, y: 4, z: 8, core: 2. Of those that a mesh axis runs over, the one named last changes fastest.
Arguments:
- embeddings: bfloat16 [65536, 1024], P(('rows', 'sub'))
- codes: int32 [64, 65536], P(None, ('rows', 'sub')), may hold values from 0 to 255
- codebook: bfloat16 [256, 1024], P(None, 'sub'), may hold values from -6 to 6
Outputs:
- rotation: float32 [1024, 1024], P('sub')
- rotated: bfloat16 [65536, 1024], P(('rows', 'sub'))
- new_codebook: float32 [256, 1024], P(None, 'sub')
All inputs are finite; a program needn't handle non-finite values.
Results may differ from a plain program's by a relative error of at most 0.0095.
Values may be sent and summed in bfloat16 or wider, within the bound.
No kernel may reach another device: no remote copies, remote signals or barrier semaphores. Data moves between devices by JAX's collectives and lax.ppermute only.
A program may use at most 64 MiB of HBM per device.

v0:
```python
import jax
import jax.numpy as jnp
from jax import lax
from jax.sharding import PartitionSpec as P

NS_STEPS = 3
coef_a = 3.4445
coef_b = -4.775
coef_c = 2.0315
frob_eps = 1e-07


def one_hot_codes(code_block, count_codes):
    levels = lax.broadcasted_iota(jnp.int32, code_block.shape + (count_codes,), 2)
    return (code_block[:, :, None] == levels).astype(jnp.bfloat16)


def decode_rows(codes, table):
    subspaces, local_rows = codes.shape
    count_codes, row_width = table.shape
    sub_width = row_width // subspaces
    codewords = table.reshape(count_codes, subspaces, sub_width)
    one_hot = one_hot_codes(codes, count_codes)
    picked = jnp.einsum("mnk,kmj->nmj", one_hot, codewords, preferred_element_type=jnp.float32)
    return picked.reshape(local_rows, row_width).astype(jnp.bfloat16)


def codeword_sums(codes, row_values, count_codes):
    subspaces, local_rows = codes.shape
    row_width = row_values.shape[1]
    sub_width = row_width // subspaces
    one_hot = one_hot_codes(codes, count_codes)
    pieces = row_values.reshape(local_rows, subspaces, sub_width)
    code_sums = jnp.einsum("mnk,nmj->kmj", one_hot, pieces, preferred_element_type=jnp.float32)
    return code_sums.reshape(count_codes, row_width)


def rows_sum(x):
    groups = lax.axis_size("rows")
    chunk = x.shape[0] // groups
    scattered = lax.all_to_all(x, "rows", split_axis=0, concat_axis=0, tiled=True)
    own = jnp.sum(scattered.reshape((groups, chunk) + x.shape[1:]), axis=0)
    spread = jnp.broadcast_to(own[None], (groups,) + own.shape).reshape(x.shape)
    return lax.all_to_all(spread, "rows", split_axis=0, concat_axis=0, tiled=True)


def panel_rows_sum(x):
    groups = lax.axis_size("rows")
    height, width = x.shape
    tiles = (
        x.reshape(height // 8, 8, 2, width // 2)
        .transpose(0, 2, 1, 3)
        .reshape(groups, 8, width // 2)
    )
    scattered = lax.all_to_all(tiles, "rows", split_axis=0, concat_axis=0, tiled=True)
    own = jnp.sum(scattered, axis=0)
    spread = jnp.broadcast_to(own[None], scattered.shape)
    gathered = lax.all_to_all(spread, "rows", split_axis=0, concat_axis=0, tiled=True)
    return (
        gathered.reshape(height // 8, 2, 8, width // 2).transpose(0, 2, 1, 3).reshape(height, width)
    )


def bdot(left, right, dims):
    return lax.dot_general(
        left.astype(jnp.bfloat16),
        right.astype(jnp.bfloat16),
        (dims, ((), ())),
        preferred_element_type=jnp.float32,
    )


def partner(x):
    count = lax.axis_size("sub")
    return lax.ppermute(x, "sub", [(i, i ^ 1) for i in range(count)])


def newton_half(z_own, z_other_half):
    own_half = z_own.astype(jnp.bfloat16)
    gram_own = bdot(own_half, own_half, ((1,), (1,)))
    gram_cross = bdot(own_half, z_other_half, ((1,), (1,)))
    gram_other = partner(gram_own.astype(jnp.bfloat16))
    own_block, cross_block = (gram_own.astype(jnp.bfloat16), gram_cross.astype(jnp.bfloat16))
    gram_rows = jnp.concatenate([own_block, cross_block], axis=1)
    quartic_left = bdot(gram_rows, gram_rows, ((1,), (1,)))
    quartic_right = bdot(own_block, cross_block, ((1,), (0,))) + bdot(
        cross_block, gram_other, ((1,), (0,))
    )
    mixer = jnp.concatenate(
        [coef_b * gram_own + coef_c * quartic_left, coef_b * gram_cross + coef_c * quartic_right],
        axis=1,
    )
    local_rows = jnp.concatenate([own_half, z_other_half], axis=0)
    return coef_a * z_own + bdot(mixer, local_rows, ((1,), (0,)))


def body(embeddings, codes, codebook):
    moved_codes = lax.all_to_all(codes, "sub", split_axis=0, concat_axis=1, tiled=True)
    table = lax.all_gather(codebook, "sub", axis=1, tiled=True)
    decoded = decode_rows(codes, table)
    partial_t = lax.dot_general(
        decoded, embeddings, (((0,), (0,)), ((), ())), preferred_element_type=jnp.float32
    )
    partial_panel = lax.psum_scatter(partial_t, "sub", scatter_dimension=1, tiled=True).T
    code_one_hot = one_hot_codes(moved_codes, table.shape[0])
    counts = jnp.sum(code_one_hot, axis=1, dtype=jnp.float32).T
    core = lax.axis_index("sub") % 2
    panel_rows = partial_panel.shape[0]
    columns = embeddings.reshape(embeddings.shape[0], -1, 2, panel_rows)
    own_columns = lax.dynamic_index_in_dim(columns, core, axis=2, keepdims=False).reshape(
        embeddings.shape[0], -1
    )
    other_columns = lax.dynamic_index_in_dim(columns, 1 - core, axis=2, keepdims=False).reshape(
        embeddings.shape[0], -1
    )
    partial_panel, moved_codes, counts, own_columns, other_columns = lax.optimization_barrier(
        (partial_panel, moved_codes, counts, own_columns, other_columns)
    )
    cross_panel = panel_rows_sum(partial_panel)
    cross = lax.all_gather(cross_panel, "sub", axis=0, tiled=True)
    width = cross.shape[1]
    frob_scale = jnp.sqrt(jnp.sum(cross * cross)) + frob_eps
    core = lax.axis_index("sub") % 2
    panel_rows = cross.shape[0] // lax.axis_size("sub")
    by_parity = cross.reshape(-1, 2, panel_rows, width)
    z_own = (
        lax.dynamic_index_in_dim(by_parity, core, axis=1, keepdims=False).reshape(-1, width)
        / frob_scale
    )
    z_other = (
        lax.dynamic_index_in_dim(by_parity, 1 - core, axis=1, keepdims=False).reshape(-1, width)
        / frob_scale
    )
    z_other_half = z_other.astype(jnp.bfloat16)
    for newton_step_index in range(NS_STEPS - 1):
        z_own = newton_half(z_own, z_other_half)
        z_other_half = partner(z_own.astype(jnp.bfloat16))
    z_own = newton_half(z_own, z_other_half)
    own_half = z_own.astype(jnp.bfloat16)
    z_other_half = partner(own_half)
    rotated = (
        jnp.dot(own_columns, own_half, preferred_element_type=jnp.float32)
        + jnp.dot(other_columns, z_other_half, preferred_element_type=jnp.float32)
    ).astype(jnp.bfloat16)
    moved_rows = lax.all_to_all(rotated, "sub", split_axis=1, concat_axis=0, tiled=True)
    code_sums = codeword_sums(moved_codes, moved_rows, table.shape[0])
    sums_width = code_sums.shape[1]
    padded_counts = jnp.pad(counts, ((0, 0), (0, sums_width - counts.shape[1])))
    totals = rows_sum(jnp.concatenate([code_sums, padded_counts], axis=1))
    code_sums, counts = (
        totals[:, :sums_width],
        totals[:, sums_width : sums_width + counts.shape[1]],
    )
    own_codebook = codebook.astype(jnp.float32)
    spread = jnp.repeat(counts, own_codebook.shape[1] // counts.shape[1], axis=1)
    new_codebook = (code_sums + own_codebook) / (spread + 1.0)
    me = lax.axis_index("sub")
    panel = lax.dynamic_index_in_dim(
        z_own.reshape(-1, panel_rows, width), me // 2, axis=0, keepdims=False
    )
    return (panel, rotated, new_codebook)


def solution(mesh):
    in_specs = (P(("rows", "sub"), None), P(None, ("rows", "sub")), P(None, "sub"))
    out_specs = (P("sub", None), P(("rows", "sub"), None), P(None, "sub"))
    return jax.shard_map(body, mesh=mesh, in_specs=in_specs, out_specs=out_specs, check_vma=False)
```

profile of v0, /device:TPU:1, one launch (start us, length us, event | category | flops | bytes accessed | tf_op | source)
XLA Modules:
  0.0 252.7 jit_solution(4950489378078883166)
XLA Ops:
  7.2 23.0 %all_gather.6 = bf16[256,1024]{0,1:T(8,128)(2,1)S(1)} all-gather(bf16[256,64]{0,1:T(8,128)(2,1)} %param.5), channel_id=1, replica_groups=mesh['rows'=16,'sub'=16] {'sub'}, dimensions={1}, use_global_device_ids=true | all-gather | bytes 557056 | tf_op jit(solution)/shard_map/all_gather | solution.py:99
  30.2 5.3 %fusion.29 = bf16[64,256,16]{1,2,0:T(8,128)(2,1)S(1)} fusion(bf16[256,64,16]{0,2,1:T(8,128)(2,1)S(1)} %bitcast.89, s32[64,256]{1,0:T(8,128)} %param.4), kind=kOutput, calls=%fused_computation.42 | convolution fusion | flops 138674176 | bytes 1114112 | tf_op jit(solution)/shard_map/mnk,kmj->nmj/dot_general | solution.py:24
  35.5 2.7 %fusion.74 = f32[1024,1024]{0,1:T(8,128)} fusion(bf16[256,1024]{0,1:T(8,128)(2,1)S(1)} %bitcast.82, bf16[256,1024]{1,0:T(8,128)(2,1)S(1)} %copy-done), kind=kOutput, calls=%fused_computation.92 | convolution fusion | flops 536870912 | bytes 5242880 | tf_op jit(solution)/shard_map/dot_general | solution.py:101
  39.8 3.8 %all-to-all-start = ((s32[16,4,256]{2,1,0:T(4,128)}), s32[16,4,256]{2,1,0:T(4,128)S(1)}, u32[]{:S(2)}, u32[]{:S(2)}) async-start(s32[16,4,256]{2,1,0:T(4,128)} %all_to_all.42), calls=%async_computation.1 | async-start | bytes 131072 | tf_op jit(solution)/shard_map/all_to_all | solution.py:98
  43.9 7.5 %all-to-all-done = s32[16,4,256]{2,1,0:T(4,128)S(1)} async-done(((s32[16,4,256]{2,1,0:T(4,128)}), s32[16,4,256]{2,1,0:T(4,128)S(1)}, u32[]{:S(2)}, u32[]{:S(2)}) %all-to-all-start) | async-done | bytes 65568 | tf_op jit(solution)/shard_map/all_to_all | solution.py:98
  51.4 6.9 %convert_reduce_fusion = f32[4,256]{1,0:T(4,128)S(1)} fusion(s32[4,4096]{1,0:T(4,128)S(1)} %bitcast.92), kind=kLoop, calls=%fused_computation.1 | loop fusion | flops 16776192 | bytes 69632 | tf_op jit(solution)/shard_map/reduce_sum | solution.py:106
  58.3 37.9 %reduce-scatter.2.cloned.1.call-done = f32[1024,64]{0,1:T(8,128)} async-done(((f32[1024,1024]{0,1:T(8,128)}), f32[1024,64]{0,1:T(8,128)}) %reduce-scatter.2.cloned.1.call-update) | async-done | bytes 262160 | tf_op jit(solution)/shard_map/reduce_scatter | solution.py:104
  96.3 13.8 %all_to_all.60 = f32[16,8,512]{2,1,0:T(8,128)S(1)} all-to-all(f32[16,8,512]{2,1,0:T(8,128)} %bitcast.91), channel_id=1, replica_groups=mesh['rows'=16,'sub'=16] {'rows'}, dimensions={0} | all-to-all | bytes 524288 | tf_op jit(solution)/shard_map/all_to_all | solution.py:55
  110.1 10.6 %all_to_all.61 = f32[16,8,512]{2,1,0:T(8,128)} all-to-all(f32[16,8,512]{2,1,0:T(8,128)S(1)} %broadcast_in_dim.6), channel_id=1, replica_groups=mesh['rows'=16,'sub'=16] {'rows'}, dimensions={0} | all-to-all | bytes 524288 | tf_op jit(solution)/shard_map/all_to_all | solution.py:58
  120.8 43.7 %all-gather.2.cloned.1.call-done = f32[1024,1024]{1,0:T(8,128)} async-done(((f32[64,1024]{1,0:T(8,128)}), f32[1024,1024]{1,0:T(8,128)}) %all-gather.2.cloned.1.call-update) | async-done | bytes 4194320 | tf_op jit(solution)/shard_map/all_gather | solution.py:120
  164.5 3.9 %multiply_reduce_fusion = f32[]{:T(128)} fusion(f32[1024,1024]{1,0:T(8,128)} %all-gather.2.cloned.1.call-done), kind=kLoop, calls=%fused_computation.9 | loop fusion | flops 2097151 | bytes 4194308 | tf_op jit(solution)/shard_map/reduce_sum | solution.py:122
  169.1 2.9 %fusion.57 = (bf16[8,1,64,1024]{3,2,1,0:T(8,128)(2,1)S(1)}, bf16[8,1,64,1024]{3,2,1,0:T(8,128)(2,1)S(1)}, f32[8,1,64,1024]{3,2,1,0:T(8,128)S(1)}) fusion(f32[]{:T(128)S(6)} %add.83, f32[8,2,64,1024]{3,2,1,0:T(8,128)} %bitcast.76, s32[]{:T(128)S(6)} %select_n.28, s32[]{:T(128)S(6)} %select_n.29), kind=kLoop, calls=%fused_computation.69 | loop fusion | flops 2621440 | bytes 8388620 | tf_op jit(solution)/shard_map/convert_element_type | solution.py:79
  175.9 1.3 fusion.67
  178.8 1.1 collective-permute-done.1
  182.5 1.3 fusion.70
  185.2 1.3 collective-permute-done.3
  189.0 1.3 fusion.73
  191.1 1.9 collective-permute-done.5
  194.5 4.6 %all-to-all-start.3 = ((bf16[256,16,64]{0,2,1:T(8,128)(2,1)}), bf16[256,16,64]{0,2,1:T(8,128)(2,1)S(1)}, u32[]{:S(2)}, u32[]{:S(2)}) async-start(bf16[256,16,64]{0,2,1:T(8,128)(2,1)} %bitcast.23), calls=%async_computation.4 | async-start | bytes 1048576 | tf_op jit(solution)/shard_map/all_to_all | solution.py:145
  199.2 17.0 %all-to-all-done.3 = bf16[256,16,64]{0,2,1:T(8,128)(2,1)S(1)} async-done(((bf16[256,16,64]{0,2,1:T(8,128)(2,1)}), bf16[256,16,64]{0,2,1:T(8,128)(2,1)S(1)}, u32[]{:S(2)}, u32[]{:S(2)}) %all-to-all-start.3) | async-done | bytes 524320 | tf_op jit(solution)/shard_map/all_to_all | solution.py:145
  216.8 3.2 %fusion.34 = f32[256,4,16]{0,2,1:T(8,128)S(1)} fusion(bf16[4096,4,16]{0,2,1:T(8,128)(2,1)S(1)} %reshape.97, s32[4,4096]{1,0:T(4,128)S(1)} %bitcast.93), kind=kOutput, calls=%fused_computation.47 | convolution fusion | flops 138412032 | bytes 655360 | tf_op jit(solution)/shard_map/mnk,nmj->kmj/dot_general | solution.py:34
  220.6 13.3 %all_to_all.62 = f32[16,16,128]{2,1,0:T(8,128)S(1)} all-to-all(f32[16,16,128]{2,1,0:T(8,128)S(1)} %pad_maximum_fusion), channel_id=1, replica_groups=mesh['rows'=16,'sub'=16] {'rows'}, dimensions={0} | all-to-all | bytes 262144 | tf_op jit(solution)/shard_map/all_to_all | solution.py:41
  234.6 3.5 %all-to-all-start.5 = ((f32[16,16,128]{2,1,0:T(8,128)}), f32[16,16,128]{2,1,0:T(8,128)S(1)}, u32[]{:S(2)}, u32[]{:S(2)}) async-start(f32[16,16,128]{2,1,0:T(8,128)} %broadcast_in_dim.7), calls=%async_computation.6 | async-start | bytes 262144 | tf_op jit(solution)/shard_map/all_to_all | solution.py:44
  239.0 5.8 %all-to-all-done.5 = f32[16,16,128]{2,1,0:T(8,128)S(1)} async-done(((f32[16,16,128]{2,1,0:T(8,128)}), f32[16,16,128]{2,1,0:T(8,128)S(1)}, u32[]{:S(2)}, u32[]{:S(2)}) %all-to-all-start.5) | async-done | bytes 131104 | tf_op jit(solution)/shard_map/all_to_all | solution.py:44
  (62 shorter events, 19.8 us)
Async XLA Ops:
  7.2 89.1 %reduce-scatter.2.cloned.1.call-start = ((), (), s32[]{:S(2)}) async-start(), calls=%async_computation.7 | async-start | bytes 4456448 | tf_op jit(solution)/shard_map/reduce_scatter | solution.py:104
  30.2 5.3 %copy-start = (bf16[256,1024]{1,0:T(8,128)(2,1)S(1)}, bf16[256,1024]{1,0:T(8,128)(2,1)}, u32[]{:S(2)}) copy-start(bf16[256,1024]{1,0:T(8,128)(2,1)} %param.3) | copy-start | bytes 1572868
  38.3 0.8 copy-start.3
  39.8 11.7 %all-to-all-start = ((s32[16,4,256]{2,1,0:T(4,128)}), s32[16,4,256]{2,1,0:T(4,128)S(1)}, u32[]{:S(2)}, u32[]{:S(2)}) async-start(s32[16,4,256]{2,1,0:T(4,128)} %all_to_all.42), calls=%async_computation.1 | async-start | bytes 131072 | tf_op jit(solution)/shard_map/all_to_all | solution.py:98
  43.6 120.9 %all-gather.2.cloned.1.call-start = ((), (), s32[]{:S(2)}) async-start(), calls=%async_computation.8 | async-start | bytes 4456448 | tf_op jit(solution)/shard_map/all_gather | solution.py:120
  173.4 2.0 collective-permute-start
  177.2 2.7 %collective-permute-start.1 = (bf16[512,1024]{1,0:T(8,128)(2,1)S(1)}, bf16[512,1024]{1,0:T(8,128)(2,1)S(1)}, u32[]{:S(2)}, u32[]{:S(2)}) collective-permute-start(bf16[512,1024]{1,0:T(8,128)(2,1)S(1)} %get-tuple-element.37), channel_id=1, source_target_pairs={{0,1},{1,0},{2,3},{3,2},{4,5},{5,4},{6,7},{7,6},{8,9},{9,8},{10,11... | collective-permute-start | bytes 3145736 | tf_op jit(solution)/shard_map/ppermute | solution.py:75
  178.4 3.6 %collective-permute-start.2 = (bf16[512,512]{0,1:T(8,128)(2,1)S(1)}, bf16[512,512]{0,1:T(8,128)(2,1)S(1)}, u32[]{:S(2)}, u32[]{:S(2)}) collective-permute-start(bf16[512,512]{0,1:T(8,128)(2,1)S(1)} %get-tuple-element.41), channel_id=1, source_target_pairs={{0,1},{1,0},{2,3},{3,2},{4,5},{5,4},{6,7},{7,6},{8,9},{9,8},{10,11... | collective-permute-start | bytes 1572872 | tf_op jit(solution)/shard_map/ppermute | solution.py:75
  183.7 2.7 %collective-permute-start.3 = (bf16[512,1024]{1,0:T(8,128)(2,1)S(1)}, bf16[512,1024]{1,0:T(8,128)(2,1)S(1)}, u32[]{:S(2)}, u32[]{:S(2)}) collective-permute-start(bf16[512,1024]{1,0:T(8,128)(2,1)S(1)} %get-tuple-element.43), channel_id=1, source_target_pairs={{0,1},{1,0},{2,3},{3,2},{4,5},{5,4},{6,7},{7,6},{8,9},{9,8},{10,11... | collective-permute-start | bytes 3145736 | tf_op jit(solution)/shard_map/ppermute | solution.py:75
  184.9 3.6 %collective-permute-start.4 = (bf16[512,512]{0,1:T(8,128)(2,1)S(1)}, bf16[512,512]{0,1:T(8,128)(2,1)S(1)}, u32[]{:S(2)}, u32[]{:S(2)}) collective-permute-start(bf16[512,512]{0,1:T(8,128)(2,1)S(1)} %get-tuple-element.47), channel_id=1, source_target_pairs={{0,1},{1,0},{2,3},{3,2},{4,5},{5,4},{6,7},{7,6},{8,9},{9,8},{10,11... | collective-permute-start | bytes 1572872 | tf_op jit(solution)/shard_map/ppermute | solution.py:75
  190.2 2.7 %collective-permute-start.5 = (bf16[512,1024]{1,0:T(8,128)(2,1)S(1)}, bf16[512,1024]{1,0:T(8,128)(2,1)S(1)}, u32[]{:S(2)}, u32[]{:S(2)}) collective-permute-start(bf16[512,1024]{1,0:T(8,128)(2,1)S(1)} %get-tuple-element.49), channel_id=1, source_target_pairs={{0,1},{1,0},{2,3},{3,2},{4,5},{5,4},{6,7},{7,6},{8,9},{9,8},{10,11... | collective-permute-start | bytes 3145736 | tf_op jit(solution)/shard_map/ppermute | solution.py:75
  193.4 1.0 copy-start.1
  194.5 21.8 %all-to-all-start.3 = ((bf16[256,16,64]{0,2,1:T(8,128)(2,1)}), bf16[256,16,64]{0,2,1:T(8,128)(2,1)S(1)}, u32[]{:S(2)}, u32[]{:S(2)}) async-start(bf16[256,16,64]{0,2,1:T(8,128)(2,1)} %bitcast.23), calls=%async_computation.4 | async-start | bytes 1048576 | tf_op jit(solution)/shard_map/all_to_all | solution.py:145
  220.0 18.1 %copy-start.2 = (bf16[256,64]{0,1:T(8,128)(2,1)S(1)}, bf16[256,64]{0,1:T(8,128)(2,1)}, u32[]{:S(2)}) copy-start(bf16[256,64]{0,1:T(8,128)(2,1)} %param.5) | copy-start | bytes 98308
  234.6 10.2 %all-to-all-start.5 = ((f32[16,16,128]{2,1,0:T(8,128)}), f32[16,16,128]{2,1,0:T(8,128)S(1)}, u32[]{:S(2)}, u32[]{:S(2)}) async-start(f32[16,16,128]{2,1,0:T(8,128)} %broadcast_in_dim.7), calls=%async_computation.6 | async-start | bytes 262144 | tf_op jit(solution)/shard_map/all_to_all | solution.py:44
Sparse Core Ops, SparseCore 0:
  38.4 57.8 reduce-scatter.1
  120.9 43.5 all-gather.1
where the time goes:
time: 254 us; the launch traced here: 253 us
  waiting for transfers between devices  117 us (46%)
  blocking collectives  60.8 us (24%)
  matrix products  25.6 us (10%)
  between operations  15.1 us (6%)
  starting transfers between devices  14.3 us (6%)
  other arithmetic  13.8 us (5%)
  local copies, waits for them, and re-layouts  6.4 us (3%)
    all_gather x1, waiting for transfers between devices, body(): cross = lax.all_gather(cross_panel, 'sub', axis=0, tiled=True)  43.7 us
    reduce_scatter x1, waiting for transfers between devices, body(): lax.psum_scatter(partial_t, 'sub', scatter_dimension=1, tiled=True)  37.9 us
    all_gather x1, blocking collectives, body(): table = lax.all_gather(codebook, 'sub', axis=1, tiled=True)  23 us
    all_to_all x1, waiting for transfers between devices, body(): lax.all_to_all(rotated, 'sub', split_axis=1, concat_axis=0, tiled=True)  17 us
    all_to_all x1, blocking collectives, panel_rows_sum(): lax.all_to_all(tiles, 'rows', split_axis=0, concat_axis=0, tiled=True)  13.8 us
    dot_general x18, matrix products, bdot(): lax.dot_general(left.astype(jnp.bfloat16), right.astype(jnp.bfloat16), (d...  13.4 us
    all_to_all x1, blocking collectives, rows_sum(): lax.all_to_all(x, 'rows', split_axis=0, concat_axis=0, tiled=True)  13.3 us
    all_to_all x1, blocking collectives, panel_rows_sum(): lax.all_to_all(spread, 'rows', split_axis=0, concat_axis=0, tiled=True)  10.6 us
  transfers between devices with their start and end apart: 11, of which 9 were waited for; matrix products, arithmetic and copies ran while one was open for 6% of the time, Pallas kernels for 0%

commit v1 on v0

--- a/solution.py
+++ b/solution.py
@@ -96,7 +96,20 @@
 
 def body(embeddings, codes, codebook):
     moved_codes = lax.all_to_all(codes, "sub", split_axis=0, concat_axis=1, tiled=True)
-    table = lax.all_gather(codebook, "sub", axis=1, tiled=True)
+    ways, here, step = (lax.axis_size("sub"), lax.axis_index("sub"), codebook.shape[1])
+    shape = [n * ways if d == 1 else n for d, n in enumerate(codebook.shape)]
+    table = lax.dynamic_update_slice_in_dim(
+        jnp.zeros(shape, codebook.dtype), codebook, here * step, axis=1
+    )
+    going_up = going_down = codebook
+    for far in range(1, ways // 2 + 1):
+        going_up = lax.ppermute(going_up, "sub", [(d, (d + 1) % ways) for d in range(ways)])
+        table = lax.dynamic_update_slice_in_dim(table, going_up, (here - far) % ways * step, axis=1)
+        if 2 * far < ways:
+            going_down = lax.ppermute(going_down, "sub", [(d, (d - 1) % ways) for d in range(ways)])
+            table = lax.dynamic_update_slice_in_dim(
+                table, going_down, (here + far) % ways * step, axis=1
+            )
     decoded = decode_rows(codes, table)
     partial_t = lax.dot_general(
         decoded, embeddings, (((0,), (0,)), ((), ())), preferred_element_type=jnp.float32

time: 254 us -> 274 us (1.079)
  starting transfers between devices: 14.3 us -> 46.7 us
  blocking collectives: 60.8 us -> 37.8 us
  waiting for transfers between devices: 117 us -> 127 us
    ppermute x0 -> x15, starting transfers between devices: none -> 26.3 us  [the longest x7 20.4 us: body(): lax.ppermute(going_down, 'sub', [(d, (d - 1) % ways) for d in range(ways)])]
    all_gather x1 -> x0, blocking collectives: 23 us -> none  [body(): table = lax.all_gather(codebook, 'sub', axis=1, tiled=True)]
    ppermute x0 -> x15, waiting for transfers between devices: none -> 9.46 us  [the longest x8 8.56 us: body(): lax.ppermute(going_up, 'sub', [(d, (d + 1) % ways) for d in range(ways)])]
    all_to_all x1, starting transfers between devices: 3.8 us -> 9.97 us  [body(): lax.all_to_all(codes, 'sub', split_axis=0, concat_axis=1, tiled=True)]
  transfers between devices with their start and end apart: 11 -> 26, of which waited for: 9 -> 22; matrix products, arithmetic and copies ran while one was open for 6% -> 6% of each run, Pallas kernels for 0% -> 0%
where the time goes in v1:
time: 274 us; the launch traced here: 273 us
  waiting for transfers between devices  127 us (46%)
  starting transfers between devices  46.7 us (17%)
  blocking collectives  37.8 us (14%)
  matrix products  25.6 us (9%)
  between operations  15.1 us (6%)
  other arithmetic  13.8 us (5%)
  local copies, waits for them, and re-layouts  7.24 us (3%)
    all_gather x1, waiting for transfers between devices, body(): cross = lax.all_gather(cross_panel, 'sub', axis=0, tiled=True)  43.9 us
    reduce_scatter x1, waiting for transfers between devices, body(): lax.psum_scatter(partial_t, 'sub', scatter_dimension=1, tiled=True)  37.9 us
    ppermute x7, starting transfers between devices, body(): lax.ppermute(going_down, 'sub', [(d, (d - 1) % ways) for d in range(ways)])  20.4 us
    all_to_all x1, waiting for transfers between devices, body(): lax.all_to_all(rotated, 'sub', split_axis=1, concat_axis=0, tiled=True)  17 us
    all_to_all x1, blocking collectives, panel_rows_sum(): lax.all_to_all(tiles, 'rows', split_axis=0, concat_axis=0, tiled=True)  13.8 us
    dot_general x18, matrix products, bdot(): lax.dot_general(left.astype(jnp.bfloat16), right.astype(jnp.bfloat16), (d...  13.4 us
    all_to_all x1, blocking collectives, rows_sum(): lax.all_to_all(x, 'rows', split_axis=0, concat_axis=0, tiled=True)  13.3 us
    all_to_all x1, blocking collectives, panel_rows_sum(): lax.all_to_all(spread, 'rows', split_axis=0, concat_axis=0, tiled=True)  10.6 us
  transfers between devices with their start and end apart: 26, of which 22 were waited for; matrix products, arithmetic and copies ran while one was open for 6% of the time, Pallas kernels for 0%

profile of v1, /device:TPU:1, one launch (start us, length us, event | category | flops | bytes accessed | tf_op | source)
XLA Modules:
  0.0 272.7 jit_solution(10190870518254151834)
XLA Ops:
  7.2 3.0 %collective-permute-start = (bf16[256,64]{0,1:T(8,128)(2,1)}, bf16[256,64]{0,1:T(8,128)(2,1)S(1)}, u32[]{:S(2)}, u32[]{:S(2)}) collective-permute-start(bf16[256,64]{0,1:T(8,128)(2,1)} %param.5), channel_id=1, source_target_pairs={{0,1},{1,2},{2,3},{3,4},{4,5},{5,6},{6,7},{7,8},{8,9},{9,10},{10,1... | collective-permute-start | bytes 98312 | tf_op jit(solution)/shard_map/ppermute | solution.py:106
  17.1 3.3 %collective-permute-start.5 = (bf16[256,64]{0,1:T(8,128)(2,1)S(1)}, bf16[256,64]{0,1:T(8,128)(2,1)S(1)}, u32[]{:S(2)}, u32[]{:S(2)}) collective-permute-start(bf16[256,64]{0,1:T(8,128)(2,1)S(1)} %collective-permute-done.3), channel_id=1, source_target_pairs={{0,15},{1,0},{2,1},{3,2},{4,3},{5,4},{6,5},{7,6},{8,7},{9,8},{10,9... | collective-permute-start | bytes 98312 | tf_op jit(solution)/shard_map/ppermute | solution.py:109
  21.3 3.7 %collective-permute-start.7 = (bf16[256,64]{0,1:T(8,128)(2,1)S(1)}, bf16[256,64]{0,1:T(8,128)(2,1)S(1)}, u32[]{:S(2)}, u32[]{:S(2)}) collective-permute-start(bf16[256,64]{0,1:T(8,128)(2,1)S(1)} %collective-permute-done.5), channel_id=1, source_target_pairs={{0,15},{1,0},{2,1},{3,2},{4,3},{5,4},{6,5},{7,6},{8,7},{9,8},{10,9... | collective-permute-start | bytes 98312 | tf_op jit(solution)/shard_map/ppermute | solution.py:109
  25.8 3.7 %collective-permute-start.9 = (bf16[256,64]{0,1:T(8,128)(2,1)S(1)}, bf16[256,64]{0,1:T(8,128)(2,1)S(1)}, u32[]{:S(2)}, u32[]{:S(2)}) collective-permute-start(bf16[256,64]{0,1:T(8,128)(2,1)S(1)} %collective-permute-done.7), channel_id=1, source_target_pairs={{0,15},{1,0},{2,1},{3,2},{4,3},{5,4},{6,5},{7,6},{8,7},{9,8},{10,9... | collective-permute-start | bytes 98312 | tf_op jit(solution)/shard_map/ppermute | solution.py:109
  30.4 3.7 %collective-permute-start.11 = (bf16[256,64]{0,1:T(8,128)(2,1)S(1)}, bf16[256,64]{0,1:T(8,128)(2,1)S(1)}, u32[]{:S(2)}, u32[]{:S(2)}) collective-permute-start(bf16[256,64]{0,1:T(8,128)(2,1)S(1)} %collective-permute-done.9), channel_id=1, source_target_pairs={{0,15},{1,0},{2,1},{3,2},{4,3},{5,4},{6,5},{7,6},{8,7},{9,8},{10,9... | collective-permute-start | bytes 98312 | tf_op jit(solution)/shard_map/ppermute | solution.py:109
  34.9 3.7 %collective-permute-start.13 = (bf16[256,64]{0,1:T(8,128)(2,1)S(1)}, bf16[256,64]{0,1:T(8,128)(2,1)S(1)}, u32[]{:S(2)}, u32[]{:S(2)}) collective-permute-start(bf16[256,64]{0,1:T(8,128)(2,1)S(1)} %collective-permute-done.11), channel_id=1, source_target_pairs={{0,15},{1,0},{2,1},{3,2},{4,3},{5,4},{6,5},{7,6},{8,7},{9,8},{10,9... | collective-permute-start | bytes 98312 | tf_op jit(solution)/shard_map/ppermute | solution.py:109
  39.5 4.4 %collective-permute-done.14 = bf16[256,64]{0,1:T(8,128)(2,1)S(1)} collective-permute-done((bf16[256,64]{0,1:T(8,128)(2,1)S(1)}, bf16[256,64]{0,1:T(8,128)(2,1)S(1)}, u32[]{:S(2)}, u32[]{:S(2)}) %collective-permute-start.14) | collective-permute-done | bytes 32800 | tf_op jit(solution)/shard_map/ppermute | solution.py:106
  43.8 5.3 %fusion.29 = bf16[64,16,256]{2,1,0:T(8,128)(2,1)S(1)} fusion(bf16[256,64,16]{0,2,1:T(8,128)(2,1)S(1)} %bitcast.89, s32[64,256]{1,0:T(8,128)} %param.4), kind=kOutput, calls=%fused_computation.42 | convolution fusion | flops 138674176 | bytes 1114112 | tf_op jit(solution)/shard_map/mnk,kmj->nmj/dot_general | solution.py:24
  49.2 2.7 %fusion.74 = f32[1024,1024]{0,1:T(8,128)} fusion(bf16[256,1024]{0,1:T(8,128)(2,1)S(1)} %bitcast.82, bf16[256,1024]{1,0:T(8,128)(2,1)S(1)} %copy-done), kind=kOutput, calls=%fused_computation.108 | convolution fusion | flops 536870912 | bytes 5242880 | tf_op jit(solution)/shard_map/dot_general | solution.py:114
  53.4 10.0 %all-to-all-start = ((s32[16,4,256]{2,1,0:T(4,128)}), s32[16,4,256]{2,1,0:T(4,128)S(1)}, u32[]{:S(2)}, u32[]{:S(2)}) async-start(s32[16,4,256]{2,1,0:T(4,128)} %all_to_all.42), calls=%async_computation.1 | async-start | bytes 131072 | tf_op jit(solution)/shard_map/all_to_all | solution.py:98
  63.7 7.5 %all-to-all-done = s32[16,4,256]{2,1,0:T(4,128)S(1)} async-done(((s32[16,4,256]{2,1,0:T(4,128)}), s32[16,4,256]{2,1,0:T(4,128)S(1)}, u32[]{:S(2)}, u32[]{:S(2)}) %all-to-all-start) | async-done | bytes 65568 | tf_op jit(solution)/shard_map/all_to_all | solution.py:98
  71.2 6.9 %convert_reduce_fusion = f32[4,256]{1,0:T(4,128)S(1)} fusion(s32[4,4096]{1,0:T(4,128)S(1)} %bitcast.92), kind=kLoop, calls=%fused_computation.1 | loop fusion | flops 16776192 | bytes 69632 | tf_op jit(solution)/shard_map/reduce_sum | solution.py:119
  78.1 37.9 %reduce-scatter.2.cloned.1.call-done = f32[1024,64]{0,1:T(8,128)} async-done(((f32[1024,1024]{0,1:T(8,128)}), f32[1024,64]{0,1:T(8,128)}) %reduce-scatter.2.cloned.1.call-update) | async-done | bytes 262160 | tf_op jit(solution)/shard_map/reduce_scatter | solution.py:117
  116.1 13.8 %all_to_all.60 = f32[16,8,512]{2,1,0:T(8,128)S(1)} all-to-all(f32[16,8,512]{2,1,0:T(8,128)} %bitcast.91), channel_id=1, replica_groups=mesh['rows'=16,'sub'=16] {'rows'}, dimensions={0} | all-to-all | bytes 524288 | tf_op jit(solution)/shard_map/all_to_all | solution.py:55
  130.0 10.6 %all_to_all.61 = f32[16,8,512]{2,1,0:T(8,128)} all-to-all(f32[16,8,512]{2,1,0:T(8,128)S(1)} %broadcast_in_dim.9), channel_id=1, replica_groups=mesh['rows'=16,'sub'=16] {'rows'}, dimensions={0} | all-to-all | bytes 524288 | tf_op jit(solution)/shard_map/all_to_all | solution.py:58
  140.6 43.9 %all-gather.2.cloned.1.call-done = f32[1024,1024]{1,0:T(8,128)} async-done(((f32[64,1024]{1,0:T(8,128)}), f32[1024,1024]{1,0:T(8,128)}) %all-gather.2.cloned.1.call-update) | async-done | bytes 4194320 | tf_op jit(solution)/shard_map/all_gather | solution.py:133
  184.5 3.9 %multiply_reduce_fusion = f32[]{:T(128)} fusion(f32[1024,1024]{1,0:T(8,128)} %all-gather.2.cloned.1.call-done), kind=kLoop, calls=%fused_computation.9 | loop fusion | flops 2097151 | bytes 4194308 | tf_op jit(solution)/shard_map/reduce_sum | solution.py:135
  189.1 2.9 %fusion.57 = (bf16[8,1,64,1024]{3,2,1,0:T(8,128)(2,1)S(1)}, bf16[8,1,64,1024]{3,2,1,0:T(8,128)(2,1)S(1)}, f32[8,1,64,1024]{3,2,1,0:T(8,128)S(1)}) fusion(f32[]{:T(128)S(6)} %add.243, f32[8,2,64,1024]{3,2,1,0:T(8,128)} %bitcast.76, s32[]{:T(128)S(6)} %select_n.167, s32[]{:T(128)S(6)} %select_n.168), kind=kLoop, calls=%fused_computation.69 | loop fusion | flops 2621440 | bytes 8388620 | tf_op jit(solution)/shard_map/convert_element_type | solution.py:79
  214.5 4.6 %all-to-all-start.3 = ((bf16[256,16,64]{0,2,1:T(8,128)(2,1)}), bf16[256,16,64]{0,2,1:T(8,128)(2,1)S(1)}, u32[]{:S(2)}, u32[]{:S(2)}) async-start(bf16[256,16,64]{0,2,1:T(8,128)(2,1)} %bitcast.23), calls=%async_computation.4 | async-start | bytes 1048576 | tf_op jit(solution)/shard_map/all_to_all | solution.py:158
  219.2 17.0 %all-to-all-done.3 = bf16[256,16,64]{0,2,1:T(8,128)(2,1)S(1)} async-done(((bf16[256,16,64]{0,2,1:T(8,128)(2,1)}), bf16[256,16,64]{0,2,1:T(8,128)(2,1)S(1)}, u32[]{:S(2)}, u32[]{:S(2)}) %all-to-all-start.3) | async-done | bytes 524320 | tf_op jit(solution)/shard_map/all_to_all | solution.py:158
  236.8 3.2 %fusion.34 = f32[256,4,16]{0,2,1:T(8,128)S(1)} fusion(bf16[4096,4,16]{0,2,1:T(8,128)(2,1)S(1)} %reshape.97, s32[4,4096]{1,0:T(4,128)S(1)} %bitcast.93), kind=kOutput, calls=%fused_computation.47 | convolution fusion | flops 138412032 | bytes 655360 | tf_op jit(solution)/shard_map/mnk,nmj->kmj/dot_general | solution.py:34
  240.6 13.3 %all_to_all.62 = f32[16,16,128]{2,1,0:T(8,128)S(1)} all-to-all(f32[16,16,128]{2,1,0:T(8,128)S(1)} %pad_maximum_fusion), channel_id=1, replica_groups=mesh['rows'=16,'sub'=16] {'rows'}, dimensions={0} | all-to-all | bytes 262144 | tf_op jit(solution)/shard_map/all_to_all | solution.py:41
  254.6 3.5 %all-to-all-start.5 = ((f32[16,16,128]{2,1,0:T(8,128)}), f32[16,16,128]{2,1,0:T(8,128)S(1)}, u32[]{:S(2)}, u32[]{:S(2)}) async-start(f32[16,16,128]{2,1,0:T(8,128)} %broadcast_in_dim.10), calls=%async_computation.6 | async-start | bytes 262144 | tf_op jit(solution)/shard_map/all_to_all | solution.py:44
  259.0 5.8 %all-to-all-done.5 = f32[16,16,128]{2,1,0:T(8,128)S(1)} async-done(((f32[16,16,128]{2,1,0:T(8,128)}), f32[16,16,128]{2,1,0:T(8,128)S(1)}, u32[]{:S(2)}, u32[]{:S(2)}) %all-to-all-start.5) | async-done | bytes 131104 | tf_op jit(solution)/shard_map/all_to_all | solution.py:44
  (108 shorter events, 39.2 us)
Async XLA Ops:
  7.2 108.9 %reduce-scatter.2.cloned.1.call-start = ((), (), s32[]{:S(2)}) async-start(), calls=%async_computation.7 | async-start | bytes 4456448 | tf_op jit(solution)/shard_map/reduce_scatter | solution.py:117
  7.2 4.4 %collective-permute-start = (bf16[256,64]{0,1:T(8,128)(2,1)}, bf16[256,64]{0,1:T(8,128)(2,1)S(1)}, u32[]{:S(2)}, u32[]{:S(2)}) collective-permute-start(bf16[256,64]{0,1:T(8,128)(2,1)} %param.5), channel_id=1, source_target_pairs={{0,1},{1,2},{2,3},{3,4},{4,5},{5,6},{6,7},{7,8},{8,9},{9,10},{10,1... | collective-permute-start | bytes 98312 | tf_op jit(solution)/shard_map/ppermute | solution.py:106
  10.2 3.6 %collective-permute-start.1 = (bf16[256,64]{0,1:T(8,128)(2,1)}, bf16[256,64]{0,1:T(8,128)(2,1)S(1)}, u32[]{:S(2)}, u32[]{:S(2)}) collective-permute-start(bf16[256,64]{0,1:T(8,128)(2,1)} %param.5), channel_id=1, source_target_pairs={{0,15},{1,0},{2,1},{3,2},{4,3},{5,4},{6,5},{7,6},{8,7},{9,8},{10,9... | collective-permute-start | bytes 98312 | tf_op jit(solution)/shard_map/ppermute | solution.py:109
  11.6 4.9 %collective-permute-start.2 = (bf16[256,64]{0,1:T(8,128)(2,1)S(1)}, bf16[256,64]{0,1:T(8,128)(2,1)S(1)}, u32[]{:S(2)}, u32[]{:S(2)}) collective-permute-start(bf16[256,64]{0,1:T(8,128)(2,1)S(1)} %collective-permute-done), channel_id=1, source_target_pairs={{0,1},{1,2},{2,3},{3,4},{4,5},{5,6},{6,7},{7,8},{8,9},{9,10},{10,1... | collective-permute-start | bytes 98312 | tf_op jit(solution)/shard_map/ppermute | solution.py:106
  13.8 3.3 %collective-permute-start.3 = (bf16[256,64]{0,1:T(8,128)(2,1)S(1)}, bf16[256,64]{0,1:T(8,128)(2,1)S(1)}, u32[]{:S(2)}, u32[]{:S(2)}) collective-permute-start(bf16[256,64]{0,1:T(8,128)(2,1)S(1)} %collective-permute-done.1), channel_id=1, source_target_pairs={{0,15},{1,0},{2,1},{3,2},{4,3},{5,4},{6,5},{7,6},{8,7},{9,8},{10,9... | collective-permute-start | bytes 98312 | tf_op jit(solution)/shard_map/ppermute | solution.py:109
  16.5 4.6 %collective-permute-start.4 = (bf16[256,64]{0,1:T(8,128)(2,1)S(1)}, bf16[256,64]{0,1:T(8,128)(2,1)S(1)}, u32[]{:S(2)}, u32[]{:S(2)}) collective-permute-start(bf16[256,64]{0,1:T(8,128)(2,1)S(1)} %collective-permute-done.2), channel_id=1, source_target_pairs={{0,1},{1,2},{2,3},{3,4},{4,5},{5,6},{6,7},{7,8},{8,9},{9,10},{10,1... | collective-permute-start | bytes 98312 | tf_op jit(solution)/shard_map/ppermute | solution.py:106
  17.1 4.1 %collective-permute-start.5 = (bf16[256,64]{0,1:T(8,128)(2,1)S(1)}, bf16[256,64]{0,1:T(8,128)(2,1)S(1)}, u32[]{:S(2)}, u32[]{:S(2)}) collective-permute-start(bf16[256,64]{0,1:T(8,128)(2,1)S(1)} %collective-permute-done.3), channel_id=1, source_target_pairs={{0,15},{1,0},{2,1},{3,2},{4,3},{5,4},{6,5},{7,6},{8,7},{9,8},{10,9... | collective-permute-start | bytes 98312 | tf_op jit(solution)/shard_map/ppermute | solution.py:109
  21.1 4.6 %collective-permute-start.6 = (bf16[256,64]{0,1:T(8,128)(2,1)S(1)}, bf16[256,64]{0,1:T(8,128)(2,1)S(1)}, u32[]{:S(2)}, u32[]{:S(2)}) collective-permute-start(bf16[256,64]{0,1:T(8,128)(2,1)S(1)} %collective-permute-done.4), channel_id=1, source_target_pairs={{0,1},{1,2},{2,3},{3,4},{4,5},{5,6},{6,7},{7,8},{8,9},{9,10},{10,1... | collective-permute-start | bytes 98312 | tf_op jit(solution)/shard_map/ppermute | solution.py:106
  21.3 4.6 %collective-permute-start.7 = (bf16[256,64]{0,1:T(8,128)(2,1)S(1)}, bf16[256,64]{0,1:T(8,128)(2,1)S(1)}, u32[]{:S(2)}, u32[]{:S(2)}) collective-permute-start(bf16[256,64]{0,1:T(8,128)(2,1)S(1)} %collective-permute-done.5), channel_id=1, source_target_pairs={{0,15},{1,0},{2,1},{3,2},{4,3},{5,4},{6,5},{7,6},{8,7},{9,8},{10,9... | collective-permute-start | bytes 98312 | tf_op jit(solution)/shard_map/ppermute | solution.py:109
  25.6 4.6 %collective-permute-start.8 = (bf16[256,64]{0,1:T(8,128)(2,1)S(1)}, bf16[256,64]{0,1:T(8,128)(2,1)S(1)}, u32[]{:S(2)}, u32[]{:S(2)}) collective-permute-start(bf16[256,64]{0,1:T(8,128)(2,1)S(1)} %collective-permute-done.6), channel_id=1, source_target_pairs={{0,1},{1,2},{2,3},{3,4},{4,5},{5,6},{6,7},{7,8},{8,9},{9,10},{10,1... | collective-permute-start | bytes 98312 | tf_op jit(solution)/shard_map/ppermute | solution.py:106
  25.8 4.6 %collective-permute-start.9 = (bf16[256,64]{0,1:T(8,128)(2,1)S(1)}, bf16[256,64]{0,1:T(8,128)(2,1)S(1)}, u32[]{:S(2)}, u32[]{:S(2)}) collective-permute-start(bf16[256,64]{0,1:T(8,128)(2,1)S(1)} %collective-permute-done.7), channel_id=1, source_target_pairs={{0,15},{1,0},{2,1},{3,2},{4,3},{5,4},{6,5},{7,6},{8,7},{9,8},{10,9... | collective-permute-start | bytes 98312 | tf_op jit(solution)/shard_map/ppermute | solution.py:109
  30.2 4.6 %collective-permute-start.10 = (bf16[256,64]{0,1:T(8,128)(2,1)S(1)}, bf16[256,64]{0,1:T(8,128)(2,1)S(1)}, u32[]{:S(2)}, u32[]{:S(2)}) collective-permute-start(bf16[256,64]{0,1:T(8,128)(2,1)S(1)} %collective-permute-done.8), channel_id=1, source_target_pairs={{0,1},{1,2},{2,3},{3,4},{4,5},{5,6},{6,7},{7,8},{8,9},{9,10},{10,1... | collective-permute-start | bytes 98312 | tf_op jit(solution)/shard_map/ppermute | solution.py:106
  30.4 4.6 %collective-permute-start.11 = (bf16[256,64]{0,1:T(8,128)(2,1)S(1)}, bf16[256,64]{0,1:T(8,128)(2,1)S(1)}, u32[]{:S(2)}, u32[]{:S(2)}) collective-permute-start(bf16[256,64]{0,1:T(8,128)(2,1)S(1)} %collective-permute-done.9), channel_id=1, source_target_pairs={{0,15},{1,0},{2,1},{3,2},{4,3},{5,4},{6,5},{7,6},{8,7},{9,8},{10,9... | collective-permute-start | bytes 98312 | tf_op jit(solution)/shard_map/ppermute | solution.py:109
  34.7 4.6 %collective-permute-start.12 = (bf16[256,64]{0,1:T(8,128)(2,1)S(1)}, bf16[256,64]{0,1:T(8,128)(2,1)S(1)}, u32[]{:S(2)}, u32[]{:S(2)}) collective-permute-start(bf16[256,64]{0,1:T(8,128)(2,1)S(1)} %collective-permute-done.10), channel_id=1, source_target_pairs={{0,1},{1,2},{2,3},{3,4},{4,5},{5,6},{6,7},{7,8},{8,9},{9,10},{10,1... | collective-permute-start | bytes 98312 | tf_op jit(solution)/shard_map/ppermute | solution.py:106
  34.9 4.6 %collective-permute-start.13 = (bf16[256,64]{0,1:T(8,128)(2,1)S(1)}, bf16[256,64]{0,1:T(8,128)(2,1)S(1)}, u32[]{:S(2)}, u32[]{:S(2)}) collective-permute-start(bf16[256,64]{0,1:T(8,128)(2,1)S(1)} %collective-permute-done.11), channel_id=1, source_target_pairs={{0,15},{1,0},{2,1},{3,2},{4,3},{5,4},{6,5},{7,6},{8,7},{9,8},{10,9... | collective-permute-start | bytes 98312 | tf_op jit(solution)/shard_map/ppermute | solution.py:109
  39.3 4.6 %collective-permute-start.14 = (bf16[256,64]{0,1:T(8,128)(2,1)S(1)}, bf16[256,64]{0,1:T(8,128)(2,1)S(1)}, u32[]{:S(2)}, u32[]{:S(2)}) collective-permute-start(bf16[256,64]{0,1:T(8,128)(2,1)S(1)} %collective-permute-done.12), channel_id=1, source_target_pairs={{0,1},{1,2},{2,3},{3,4},{4,5},{5,6},{6,7},{7,8},{8,9},{9,10},{10,1... | collective-permute-start | bytes 98312 | tf_op jit(solution)/shard_map/ppermute | solution.py:106
  53.4 17.9 %all-to-all-start = ((s32[16,4,256]{2,1,0:T(4,128)}), s32[16,4,256]{2,1,0:T(4,128)S(1)}, u32[]{:S(2)}, u32[]{:S(2)}) async-start(s32[16,4,256]{2,1,0:T(4,128)} %all_to_all.42), calls=%async_computation.1 | async-start | bytes 131072 | tf_op jit(solution)/shard_map/all_to_all | solution.py:98
  63.4 121.1 %all-gather.2.cloned.1.call-start = ((), (), s32[]{:S(2)}) async-start(), calls=%async_computation.8 | async-start | bytes 4456448 | tf_op jit(solution)/shard_map/all_gather | solution.py:133
  197.3 2.7 %collective-permute-start.16 = (bf16[512,1024]{1,0:T(8,128)(2,1)S(1)}, bf16[512,1024]{1,0:T(8,128)(2,1)S(1)}, u32[]{:S(2)}, u32[]{:S(2)}) collective-permute-start(bf16[512,1024]{1,0:T(8,128)(2,1)S(1)} %get-tuple-element.37), channel_id=1, source_target_pairs={{0,1},{1,0},{2,3},{3,2},{4,5},{5,4},{6,7},{7,6},{8,9},{9,8},{10,11... | collective-permute-start | bytes 3145736 | tf_op jit(solution)/shard_map/ppermute | solution.py:75
  198.4 3.6 %collective-permute-start.17 = (bf16[512,512]{0,1:T(8,128)(2,1)S(1)}, bf16[512,512]{0,1:T(8,128)(2,1)S(1)}, u32[]{:S(2)}, u32[]{:S(2)}) collective-permute-start(bf16[512,512]{0,1:T(8,128)(2,1)S(1)} %get-tuple-element.41), channel_id=1, source_target_pairs={{0,1},{1,0},{2,3},{3,2},{4,5},{5,4},{6,7},{7,6},{8,9},{9,8},{10,11... | collective-permute-start | bytes 1572872 | tf_op jit(solution)/shard_map/ppermute | solution.py:75
  203.8 2.7 %collective-permute-start.18 = (bf16[512,1024]{1,0:T(8,128)(2,1)S(1)}, bf16[512,1024]{1,0:T(8,128)(2,1)S(1)}, u32[]{:S(2)}, u32[]{:S(2)}) collective-permute-start(bf16[512,1024]{1,0:T(8,128)(2,1)S(1)} %get-tuple-element.43), channel_id=1, source_target_pairs={{0,1},{1,0},{2,3},{3,2},{4,5},{5,4},{6,7},{7,6},{8,9},{9,8},{10,11... | collective-permute-start | bytes 3145736 | tf_op jit(solution)/shard_map/ppermute | solution.py:75
  204.9 3.6 %collective-permute-start.19 = (bf16[512,512]{0,1:T(8,128)(2,1)S(1)}, bf16[512,512]{0,1:T(8,128)(2,1)S(1)}, u32[]{:S(2)}, u32[]{:S(2)}) collective-permute-start(bf16[512,512]{0,1:T(8,128)(2,1)S(1)} %get-tuple-element.47), channel_id=1, source_target_pairs={{0,1},{1,0},{2,3},{3,2},{4,5},{5,4},{6,7},{7,6},{8,9},{9,8},{10,11... | collective-permute-start | bytes 1572872 | tf_op jit(solution)/shard_map/ppermute | solution.py:75
  214.5 21.8 %all-to-all-start.3 = ((bf16[256,16,64]{0,2,1:T(8,128)(2,1)}), bf16[256,16,64]{0,2,1:T(8,128)(2,1)S(1)}, u32[]{:S(2)}, u32[]{:S(2)}) async-start(bf16[256,16,64]{0,2,1:T(8,128)(2,1)} %bitcast.23), calls=%async_computation.4 | async-start | bytes 1048576 | tf_op jit(solution)/shard_map/all_to_all | solution.py:158
  254.6 10.2 %all-to-all-start.5 = ((f32[16,16,128]{2,1,0:T(8,128)}), f32[16,16,128]{2,1,0:T(8,128)S(1)}, u32[]{:S(2)}, u32[]{:S(2)}) async-start(f32[16,16,128]{2,1,0:T(8,128)} %broadcast_in_dim.10), calls=%async_computation.6 | async-start | bytes 262144 | tf_op jit(solution)/shard_map/all_to_all | solution.py:44
  (6 other events, 30.0 us)
Sparse Core Ops, SparseCore 0:
  52.1 63.9 reduce-scatter.1
  140.7 43.7 all-gather.1
